TPU v7x, 256 devices: a whole 4x4x8 slice. The times are simulated.
256 devices in a mesh: cfg: 2 (over z_lo), seq: 16 (over z_hi, x), wblk: 8 (over y, core).
Axes of the slice: x: 4, y: 4, z: 8 (z_hi: 4, z_lo: 2; z = z_hi * 2 + z_lo), core: 2. Of those that a mesh axis runs over, the one named last changes fastest.
Arguments:
- text_tokens: bfloat16 [2, 2, 512, 3072], P('cfg', None, 'seq', 'wblk'), may hold values from -16 to 16
- image_tokens: bfloat16 [2, 4096, 3072], P(None, 'seq', 'wblk'), may hold values from -16 to 16
- pooled_vector: float32 [2, 3072], P('cfg', 'seq'), may hold values from -6 to 6
- mod_weight: bfloat16 [3072, 3, 3072], P('seq', None, 'wblk'), may hold values from -0.109375 to 0.109375
- qkv_weight: bfloat16 [3072, 3, 16, 128], P('seq', None, 'wblk'), may hold values from -0.109375 to 0.109375
- up_weight: bfloat16 [3072, 6144], P('seq', 'wblk'), may hold values from -0.109375 to 0.109375
- query_gain: float32 [128], replicated, may hold values from 0.6 to 10
- key_gain: float32 [128], replicated, may hold values from 0.6 to 10
- attn_weight: bfloat16 [2048, 3072], P('wblk', 'seq'), may hold values from -0.125 to 0.125
- down_weight: bfloat16 [6144, 3072], P('wblk', 'seq'), may hold values from -0.078125 to 0.078125
- lengths: int32 [2], replicated, may hold values from 1 to 512, as said below
- timestep: int32 [1], replicated, may hold values from 0 to 27
Outputs:
- text_out: bfloat16 [2, 2, 512, 3072], P('cfg', None, 'seq', 'wblk')
- velocity: float32 [2, 4096, 3072], P('cfg', 'seq', 'wblk')
- new_image: float32 [2, 4096, 3072], P('cfg', 'seq', 'wblk')
Inputs may be any that keep to these rules, and one draw needn't show every extreme that they name: `lengths`: some prompt has all 512 text tokens live in every draw.
All inputs are finite; a program needn't handle non-finite values.
Results may differ from a plain program's by a relative error of at most 0.025.
Values may be sent and summed in bfloat16 or wider, within the bound.
No kernel may reach another device: no remote copies, remote signals or barrier semaphores. Data moves between devices by JAX's collectives and lax.ppermute only.
A program may use at most 128 MiB of HBM per device.

v0:
```python
import math
import jax
import jax.numpy as jnp
from jax import lax
from jax.sharding import PartitionSpec as P

D = 3072
HD = 128
GRID = 64
STEPS = 28
epsilon = 1e-06
guidance = 3.5
time_shift = 3.0
rope_theta = 10000.0


def plan(timestep):
    step_index = timestep[0].astype(jnp.float32)
    time_now = 1.0 - step_index / STEPS
    time_next = 1.0 - (step_index + 1.0) / STEPS
    sigma_now = time_shift * time_now / (1.0 + (time_shift - 1.0) * time_now)
    sigma_next = time_shift * time_next / (1.0 + (time_shift - 1.0) * time_next)
    return (sigma_now, sigma_next - sigma_now)


def time_embedding(sigma_now, dim_count):
    halfwidth = dim_count // 2
    frequency = jnp.exp(-math.log(10000.0) * jnp.arange(halfwidth, dtype=jnp.float32) / halfwidth)
    angles = 1000.0 * sigma_now * frequency
    return jnp.concatenate([jnp.cos(angles), jnp.sin(angles)])


def inverse_freq(dim_count):
    return rope_theta ** (-jnp.arange(0, dim_count, 2, dtype=jnp.float32) / dim_count)


def rotary_angles(height_pos, width_pos):
    still_dims = HD // 8
    axis_dims = (HD - still_dims) // 2
    return jnp.concatenate(
        [
            jnp.zeros((height_pos.shape[0], still_dims // 2), jnp.float32),
            height_pos[:, None] * inverse_freq(axis_dims)[None],
            width_pos[:, None] * inverse_freq(axis_dims)[None],
        ],
        axis=1,
    )


def rotate(vectors, angles):
    paired_dims = vectors.reshape(vectors.shape[:-1] + (HD // 2, 2))
    cosine_table = jnp.cos(angles)[:, None, :]
    sine_table = jnp.sin(angles)[:, None, :]
    first_part = paired_dims[..., 0]
    second_part = paired_dims[..., 1]
    turned = jnp.stack(
        [
            first_part * cosine_table - second_part * sine_table,
            first_part * sine_table + second_part * cosine_table,
        ],
        axis=-1,
    )
    return turned.reshape(vectors.shape)


def head_norm(vectors, gain_vector):
    return (
        vectors
        * lax.rsqrt(jnp.mean(vectors * vectors, axis=-1, keepdims=True) + epsilon)
        * gain_vector
    )


def input_folder(source, pieces):
    width_rows = pieces[0].shape[0]
    first_total = jnp.dot(
        source, pieces[0].reshape(width_rows, -1), preferred_element_type=jnp.float32
    )
    second_total = jnp.dot(source, pieces[1], preferred_element_type=jnp.float32)
    return (first_total, second_total)


def output_folder(attended, activated, pieces):
    block_cols = jnp.dot(attended, pieces[0], preferred_element_type=jnp.float32)
    block_cols = block_cols + jnp.dot(activated, pieces[1], preferred_element_type=jnp.float32)
    return block_cols


def shards(
    text_tokens,
    image_tokens,
    pooled_vector,
    mod_weight,
    qkv_weight,
    up_weight,
    query_gain,
    key_gain,
    attn_weight,
    down_weight,
    lengths,
    timestep,
):
    seq_pos = lax.axis_index("seq")
    cfg_pos = lax.axis_index("cfg")
    prompts = image_tokens.shape[0]
    image_rows = image_tokens.shape[1]
    text_rows = text_tokens.shape[2]
    local_len = text_rows + image_rows
    dim_local = image_tokens.shape[2]
    dim_seq = pooled_vector.shape[1]
    heads_local = qkv_weight.shape[2]
    row_count = prompts * local_len
    sigma_now, step_size = plan(timestep)
    embedded = lax.dynamic_slice_in_dim(time_embedding(sigma_now, D), seq_pos * dim_seq, dim_seq)
    cond_vec = jax.nn.silu(pooled_vector[0] + embedded).astype(jnp.bfloat16)[None]
    mod_terms = jnp.dot(
        cond_vec, mod_weight.reshape(dim_seq, 3 * dim_local), preferred_element_type=jnp.float32
    )
    modulation = lax.psum(mod_terms.reshape(3, dim_local), "seq")
    local_rows = jnp.concatenate([text_tokens[0], image_tokens], axis=1)
    hidden = local_rows.astype(jnp.float32)
    totals, squares = lax.psum(
        (jnp.sum(hidden, axis=-1), jnp.sum(hidden * hidden, axis=-1)), "wblk"
    )
    average = (totals / D)[..., None]
    variance = (squares / D)[..., None] - average * average
    normed = (
        (hidden - average) * lax.rsqrt(variance + epsilon) * (1.0 + modulation[1]) + modulation[0]
    ).astype(jnp.bfloat16)
    gathered = lax.all_gather(normed, "wblk", axis=2, tiled=True)
    token_rows = gathered.reshape(row_count, D)
    projected, mlp_units = input_folder(
        token_rows,
        (
            lax.all_gather(qkv_weight, "seq", axis=0, tiled=True),
            lax.all_gather(up_weight, "seq", axis=0, tiled=True),
        ),
    )
    projected = projected.reshape(prompts, local_len, 3, heads_local, HD)
    image_index = seq_pos * image_rows + jnp.arange(image_rows, dtype=jnp.int32)
    height_pos = jnp.concatenate(
        [jnp.zeros((text_rows,), jnp.float32), (image_index // GRID).astype(jnp.float32)]
    )
    width_pos = jnp.concatenate(
        [jnp.zeros((text_rows,), jnp.float32), (image_index % GRID).astype(jnp.float32)]
    )
    angles = rotary_angles(height_pos, width_pos)
    queries = rotate(head_norm(projected[:, :, 0], query_gain), angles).astype(jnp.bfloat16)
    key_rows = rotate(head_norm(projected[:, :, 1], key_gain), angles).astype(jnp.bfloat16)
    values = projected[:, :, 2].astype(jnp.bfloat16)
    scale_factor = HD ** (-0.5)
    running_max = jnp.full((prompts, heads_local, local_len), -1e30, jnp.float32)
    key_piece = lax.all_gather(key_rows, "seq", axis=1, tiled=True)
    value_piece = lax.all_gather(values, "seq", axis=1, tiled=True)
    width_keys = key_piece.shape[1]
    where_global = jnp.arange(width_keys, dtype=jnp.int32)
    shard_index = where_global // local_len
    within = where_global % local_len
    text_index = shard_index * text_rows + within
    key_live = (within >= text_rows)[None, :] | (text_index[None, :] < lengths[:, None])
    scores = (
        jnp.einsum("pqhd,pkhd->phqk", queries, key_piece, preferred_element_type=jnp.float32)
        * scale_factor
    )
    scores = jnp.where(key_live[:, None, None, :], scores, -1e30)
    new_max = jnp.maximum(running_max, jnp.max(scores, axis=-1))
    weights = jnp.exp(scores - new_max[..., None])
    denominator = jnp.sum(weights, axis=-1)
    numerator = jnp.einsum(
        "phqk,pkhd->phqd",
        weights.astype(jnp.bfloat16),
        value_piece,
        preferred_element_type=jnp.float32,
    )
    running_max, denominator, numerator = (new_max, denominator, numerator)
    attended = (numerator / denominator[..., None]).astype(jnp.bfloat16)
    attended = attended.transpose(0, 2, 1, 3).reshape(row_count, heads_local * HD)
    activated = jax.nn.gelu(mlp_units, approximate=True).astype(jnp.bfloat16)
    branch_terms = output_folder(
        attended,
        activated,
        (
            lax.all_gather(attn_weight, "seq", axis=1, tiled=True),
            lax.all_gather(down_weight, "seq", axis=1, tiled=True),
        ),
    )
    branch = lax.psum_scatter(
        branch_terms.reshape(prompts, local_len, D).astype(jnp.bfloat16),
        "wblk",
        scatter_dimension=2,
        tiled=True,
    ).astype(jnp.float32)
    layer_out = hidden + modulation[2] * branch
    text_out = layer_out[:, :text_rows].astype(jnp.bfloat16)[None]
    image_out = layer_out[:, text_rows:]
    paired = lax.all_to_all(
        image_out[:, None].astype(jnp.bfloat16), "cfg", split_axis=0, concat_axis=1, tiled=True
    ).astype(jnp.float32)
    velocity = paired[:, 1] + guidance * (paired[:, 0] - paired[:, 1])
    own_prompts = prompts // 2
    latent = lax.dynamic_slice_in_dim(image_tokens, cfg_pos * own_prompts, own_prompts, 0).astype(
        jnp.float32
    )
    new_image = latent + step_size * velocity
    return (text_out, velocity, new_image)


def solution(mesh):
    in_specs = (
        P("cfg", None, "seq", "wblk"),
        P(None, "seq", "wblk"),
        P("cfg", "seq"),
        P("seq", None, "wblk"),
        P("seq", None, "wblk", None),
        P("seq", "wblk"),
        P(),
        P(),
        P("wblk", "seq"),
        P("wblk", "seq"),
        P(),
        P(),
    )
    out_specs = (P("cfg", None, "seq", "wblk"), P("cfg", "seq", "wblk"), P("cfg", "seq", "wblk"))
    return jax.shard_map(shards, mesh=mesh, in_specs=in_specs, out_specs=out_specs, check_vma=False)
```

profile of v0, /device:TPU:2, one launch (start us, length us, event | category | flops | bytes accessed | tf_op | source)
XLA Modules:
  0.0 606.9 jit_solution(16747836014548433341)
XLA Ops:
  11.0 15.1 %all-reduce.2 = (f32[2,288]{1,0:T(2,128)S(1)}, f32[2,288]{1,0:T(2,128)S(1)}) all-reduce(f32[2,288]{1,0:T(2,128)S(1)} %get-tuple-element.6, f32[2,288]{1,0:T(2,128)S(1)} %get-tuple-element.5), channel_id=1, replica_groups=mesh['cfg'=2,'seq'=16,'wblk'=8] {'wblk'}, use_global_device_ids=true, to_apply=%region_4.5 | all-reduce | flops 1152 | bytes 9216 | tf_op jit(solution)/shard_map/psum | solution.py:122
  26.1 46.2 %psum.21 = f32[3,384]{1,0:T(4,128)S(1)} all-reduce(f32[3,384]{1,0:T(4,128)S(1)} %bitcast.105), channel_id=1, replica_groups=mesh['cfg'=2,'seq'=16,'wblk'=8] {'seq'}, use_global_device_ids=true, to_apply=%region_0.1 | all-reduce | flops 1152 | bytes 9216 | tf_op jit(solution)/shard_map/psum | solution.py:119
  72.4 2.0 fusion.36
  78.1 13.8 %all-gather.11.cloned.1.call-done = bf16[3072,3,2,128]{3,2,1,0:T(2,128)(2,1)} async-done(((bf16[192,3,2,128]{3,2,1,0:T(2,128)(2,1)}), bf16[3072,3,2,128]{3,2,1,0:T(2,128)(2,1)}) %all-gather.11.cloned.1.call-update) | async-done | bytes 4718608 | tf_op jit(solution)/shard_map/all_gather | solution.py:135
  91.9 12.5 %copy.34 = bf16[3072,3,2,128]{0,3,2,1:T(8,128)(2,1)} copy(bf16[3072,3,2,128]{3,2,1,0:T(2,128)(2,1)} %all-gather.11.cloned.1.call-done) | data formatting | bytes 9437184 | tf_op jit(solution)/shard_map/reshape | solution.py:77
  104.4 23.5 %all-gather.9.cloned.1.call-done = bf16[2,288,3072]{2,1,0:T(8,128)(2,1)} async-done(((bf16[2,288,384]{2,1,0:T(8,128)(2,1)}), bf16[2,288,3072]{2,1,0:T(8,128)(2,1)}) %all-gather.9.cloned.1.call-update) | async-done | bytes 3538960 | tf_op jit(solution)/shard_map/all_gather | solution.py:130
  127.9 6.8 %fusion.6 = f32[2,288,3,2,128]{4,1,3,2,0:T(8,128)S(1)} fusion(bf16[3072,3,2,128]{0,3,2,1:T(8,128)(2,1)} %copy.34, bf16[2,288,3072]{2,1,0:T(8,128)(2,1)} %all-gather.9.cloned.1.call-done), kind=kOutput, calls=%fused_computation.8 | convolution fusion | flops 2717908992 | bytes 10027008 | tf_op jit(solution)/shard_map/dot_general | solution.py:76
  140.2 1.8 slice.102
  143.8 64.8 %all-gather.17.cloned.1.call-done = bf16[3072,768]{1,0:T(8,128)(2,1)} async-done(((bf16[192,768]{1,0:T(8,128)(2,1)}), bf16[3072,768]{1,0:T(8,128)(2,1)}) %all-gather.17.cloned.1.call-update) | async-done | bytes 4718608 | tf_op jit(solution)/shard_map/all_gather | solution.py:136
  208.6 82.8 %all-gather.19.cloned.1.call-done = bf16[768,3072]{0,1:T(8,128)(2,1)} async-done(((bf16[768,192]{0,1:T(8,128)(2,1)}), bf16[768,3072]{0,1:T(8,128)(2,1)}) %all-gather.19.cloned.1.call-update) | async-done | bytes 4718608 | tf_op jit(solution)/shard_map/all_gather | solution.py:184
  291.5 15.0 %fusion.39 = f32[576,3072]{1,0:T(8,128)} fusion(bf16[768,3072]{0,1:T(8,128)(2,1)} %all-gather.19.cloned.1.call-done, bf16[576,3072]{1,0:T(8,128)(2,1)} %bitcast.108, bf16[3072,768]{1,0:T(8,128)(2,1)} %all-gather.17.cloned.1.call-done), kind=kOutput, calls=%fused_computation.34 | convolution fusion | flops 5439799296 | bytes 20054016 | tf_op jit(solution)/shard_map/dot_general | solution.py:85
  306.5 68.4 %all-gather.13.cloned.1.call-done = bf16[2,4608,2,128]{3,1,2,0:T(8,128)(2,1)} async-done(((bf16[2,288,2,128]{3,1,2,0:T(8,128)(2,1)}), bf16[2,4608,2,128]{3,1,2,0:T(8,128)(2,1)}) %all-gather.13.cloned.1.call-update) | async-done | bytes 4718608 | tf_op jit(solution)/shard_map/all_gather | solution.py:153
  374.9 13.5 %fusion = (f32[2,2,288]{2,1,0:T(2,128)S(1)}, f32[2,2,288,4608]{3,2,1,0:T(8,128)}) fusion(pred[2,4608]{1,0:T(4,128)(4,1)S(1)} %compare_or_fusion, bf16[2,4608,2,128]{3,1,2,0:T(8,128)(2,1)} %all-gather.13.cloned.1.call-done, bf16[2,288,2,128]{1,2,3,0:T(2,128)(2,1)S(1)} %bitcast.100), kind=kOutput, calls=%fused_computation.2 | convolution fusion | flops 1374878592 | bytes 26260992 | tf_op jit(solution)/shard_map/pqhd,pkhd->phqk/dot_general | solution.py:162
  388.4 10.3 %fusion.1 = f32[2,2,288]{2,1,0:T(2,128)S(1)} fusion(f32[2,2,288,4608]{3,2,1,0:T(8,128)} %get-tuple-element.29, f32[2,2,288]{2,1,0:T(2,128)S(1)} %broadcast_maximum_fusion, pred[2,4608]{1,0:T(4,128)(4,1)S(1)} %compare_or_fusion), kind=kLoop, calls=%fused_computation.3 | loop fusion | flops 21232512 | bytes 21252096 | tf_op jit(solution)/shard_map/reduce_sum | solution.py:168
  398.7 59.5 %all-gather.21.cloned.1.call-done = bf16[2,4608,1,2,128]{4,1,3,2,0:T(8,128)(2,1)} async-done(((bf16[2,288,1,2,128]{4,1,3,2,0:T(8,128)(2,1)}), bf16[2,4608,1,2,128]{4,1,3,2,0:T(8,128)(2,1)}) %all-gather.21.cloned.1.call-update) | async-done | bytes 4718608 | tf_op jit(solution)/shard_map/all_gather | solution.py:154
  458.3 10.9 %fusion.28 = bf16[2,288,2,128]{3,1,2,0:T(8,128)(2,1)S(1)} fusion(bf16[2,4608,1,2,128]{4,1,3,2,0:T(8,128)(2,1)} %all-gather.21.cloned.1.call-done, f32[2,2,288,4608]{3,2,1,0:T(8,128)} %get-tuple-element.29, f32[2,2,288]{2,1,0:T(2,128)S(1)} %broadcast_maximum_fusion, pred[2,4608]{1,0:T(4,128)(4,1)S(1)} %compare_or_fusion, f32[2,288,2]{1,2,0:T(2,128)S(1)} %bitcast.106), kind=kOutput, calls=%fused_computation.27 | convolution fusion | flops 1380483072 | bytes 26265600 | tf_op jit(solution)/shard_map/phqk,pkhd->phqd/dot_general | solution.py:169
  469.5 50.2 %all-gather.15.cloned.1.call-done = bf16[256,3072]{0,1:T(8,128)(2,1)} async-done(((bf16[256,192]{0,1:T(8,128)(2,1)}), bf16[256,3072]{0,1:T(8,128)(2,1)}) %all-gather.15.cloned.1.call-update) | async-done | bytes 1572880 | tf_op jit(solution)/shard_map/all_gather | solution.py:183
  519.6 6.4 %add_convert_fusion = bf16[576,3072]{1,0:T(8,128)(2,1)} fusion(f32[576,3072]{1,0:T(8,128)} %fusion.39, bf16[256,3072]{0,1:T(8,128)(2,1)} %all-gather.15.cloned.1.call-done, bf16[72,8,2,128]{3,2,1,0:T(2,128)(2,1)S(1)} %bitcast.101), kind=kOutput, calls=%fused_computation.7 | convolution fusion | flops 909508608 | bytes 12484608 | tf_op jit(solution)/shard_map/dot_general | solution.py:84
  526.0 12.3 %copy.35 = bf16[2,288,3072]{1,0,2:T(2,128)(2,1)} copy(bf16[2,288,3072]{2,1,0:T(8,128)(2,1)} %bitcast.95) | data formatting | bytes 7077888
  538.3 10.2 %reshape.323 = bf16[3072,576]{1,0:T(8,128)(2,1)} reshape(bf16[3072,2,288]{2,1,0:T(2,128)(2,1)} %bitcast.94) | data formatting | bytes 7077888
  548.5 37.4 %reduce-scatter.4.cloned.1.call-done = bf16[384,576]{1,0:T(8,128)(2,1)} async-done(((bf16[3072,576]{1,0:T(8,128)(2,1)}), bf16[384,576]{1,0:T(8,128)(2,1)}) %reduce-scatter.4.cloned.1.call-update) | async-done | bytes 442384
  585.9 2.1 reshape.324
  589.7 3.5 all-to-all-start
  593.8 5.2 all-to-all-done
  (68 shorter events, 17.4 us)
Async XLA Ops:
  7.2 2.3 copy-start
  7.2 84.7 %all-gather.11.cloned.1.call-start = ((), (), s32[]{:S(2)}) async-start(), calls=%async_computation.3 | async-start | bytes 5013504 | tf_op jit(solution)/shard_map/all_gather | solution.py:135
  7.9 120.0 %all-gather.9.cloned.1.call-start = ((), (), s32[]{:S(2)}) async-start(), calls=%async_computation.2 | async-start | bytes 3981312 | tf_op jit(solution)/shard_map/all_gather | solution.py:130
  74.4 134.2 %all-gather.17.cloned.1.call-start = ((), (), s32[]{:S(2)}) async-start(), calls=%async_computation.6 | async-start | bytes 5013504 | tf_op jit(solution)/shard_map/all_gather | solution.py:136
  75.2 216.3 %all-gather.19.cloned.1.call-start = ((), (), s32[]{:S(2)}) async-start(), calls=%async_computation.7 | async-start | bytes 5013504 | tf_op jit(solution)/shard_map/all_gather | solution.py:184
  75.7 299.1 %all-gather.13.cloned.1.call-start = ((), (), s32[]{:S(2)}) async-start(), calls=%async_computation.4 | async-start | bytes 5013504 | tf_op jit(solution)/shard_map/all_gather | solution.py:153
  134.6 1.2 copy-start.3
  136.4 6.7 %copy-start.5 = (s32[2]{0:T(128)S(1)}, s32[2]{0:T(128)}, u32[]{:S(2)}) copy-start(s32[2]{0:T(128)} %param.22) | copy-start | bytes 28
  140.2 318.1 %all-gather.21.cloned.1.call-start = ((), (), s32[]{:S(2)}) async-start(), calls=%async_computation.8 | async-start | bytes 5013504 | tf_op jit(solution)/shard_map/all_gather | solution.py:154
  142.1 377.6 %all-gather.15.cloned.1.call-start = ((), (), s32[]{:S(2)}) async-start(), calls=%async_computation.5 | async-start | bytes 1671168 | tf_op jit(solution)/shard_map/all_gather | solution.py:183
  142.8 443.1 %reduce-scatter.4.cloned.1.call-start = ((), (), s32[]{:S(2)}) async-start(), calls=%async_computation.9 | async-start | bytes 4423680
  548.5 40.2 %copy-start.2 = (bf16[2,256,384]{2,1,0:T(8,128)(2,1)S(1)}, bf16[2,256,384]{2,1,0:T(8,128)(2,1)}, u32[]{:S(2)}) copy-start(bf16[2,256,384]{2,1,0:T(8,128)(2,1)} %param.13) | copy-start | bytes 1179652
  548.5 40.3 %copy-start.4 = (bf16[1,2,32,384]{3,2,1,0:T(8,128)(2,1)S(1)}, bf16[1,2,32,384]{3,2,1,0:T(8,128)(2,1)}, u32[]{:S(2)}) copy-start(bf16[1,2,32,384]{3,2,1,0:T(8,128)(2,1)} %param.12) | copy-start | bytes 147460
  548.5 51.5 %copy-start.1 = (bf16[192,3,384]{2,0,1:T(8,128)(2,1)S(1)}, bf16[192,3,384]{2,0,1:T(8,128)(2,1)}, u32[]{:S(2)}) copy-start(bf16[192,3,384]{2,0,1:T(8,128)(2,1)} %param.15) | copy-start | bytes 1327108
  589.7 9.3 %all-to-all-start = ((bf16[2,1,256,384]{3,2,1,0:T(8,128)(2,1)}), bf16[2,1,256,384]{3,2,1,0:T(8,128)(2,1)S(1)}, u32[]{:S(2)}, u32[]{:S(2)}) async-start(bf16[2,1,256,384]{3,2,1,0:T(8,128)(2,1)} %slice_bitcast_fusion.2), calls=%async_computation | async-start | bytes 786432 | tf_op jit(solution)/shard_map/all_to_all | solution.py:196
Sparse Core Ops, SparseCore 0:
  10.4 81.3 all-gather.10
  93.7 34.1 all-gather.8
  130.3 78.2 all-gather.16
  210.9 80.5 all-gather.18
  294.3 80.5 all-gather.12
  377.7 80.5 all-gather.20
  460.7 58.8 all-gather.14
  548.6 37.2 reduce-scatter.3
where the time goes:
time: 608 us; the launch traced here: 607 us
  waiting for transfers between devices  408 us (67%)
  blocking collectives  61.3 us (10%)
  matrix products  52.8 us (9%)
  local copies, waits for them, and re-layouts  45.8 us (8%)
  other arithmetic  19.5 us (3%)
  between operations  15.2 us (2%)
    all_gather x1, waiting for transfers between devices, shards(): lax.all_gather(down_weight, 'seq', axis=1, tiled=True)  82.8 us
    all_gather x1, waiting for transfers between devices, shards(): key_piece = lax.all_gather(key_rows, 'seq', axis=1, tiled=True)  68.4 us
    all_gather x1, waiting for transfers between devices, shards(): lax.all_gather(up_weight, 'seq', axis=0, tiled=True)  64.8 us
    all_gather x1, waiting for transfers between devices, shards(): value_piece = lax.all_gather(values, 'seq', axis=1, tiled=True)  59.5 us
    all_gather x1, waiting for transfers between devices, shards(): lax.all_gather(attn_weight, 'seq', axis=1, tiled=True)  50.2 us
    psum x1, blocking collectives, shards(): modulation = lax.psum(mod_terms.reshape(3, dim_local), 'seq')  46.2 us
    unnamed x9, waiting for transfers between devices  40 us
    unnamed x16, local copies, waits for them, and re-layouts  26 us
  transfers between devices with their start and end apart: 9, of which 9 were waited for; matrix products, arithmetic and copies ran while one was open for 14% of the time, Pallas kernels for 0%

commit v1 on v0

--- a/solution.py
+++ b/solution.py
@@ -127,7 +127,23 @@
     normed = (
         (hidden - average) * lax.rsqrt(variance + epsilon) * (1.0 + modulation[1]) + modulation[0]
     ).astype(jnp.bfloat16)
-    gathered = lax.all_gather(normed, "wblk", axis=2, tiled=True)
+    peers, index, width = (lax.axis_size("wblk"), lax.axis_index("wblk"), normed.shape[2])
+    forward = [(i, (i + 1) % peers) for i in range(peers)]
+    behind = [(i, (i - 1) % peers) for i in range(peers)]
+    gathered = jnp.zeros((*normed.shape[:2], peers * width, *normed.shape[2 + 1 :]), normed.dtype)
+    gathered = lax.dynamic_update_slice_in_dim(gathered, normed, index * width, axis=2)
+    from_left = from_right = normed
+    half = peers // 2
+    for step in range(1, half + 1):
+        from_left = lax.ppermute(from_left, "wblk", forward)
+        gathered = lax.dynamic_update_slice_in_dim(
+            gathered, from_left, (index - step) % peers * width, axis=2
+        )
+        if step < peers - half:
+            from_right = lax.ppermute(from_right, "wblk", behind)
+            gathered = lax.dynamic_update_slice_in_dim(
+                gathered, from_right, (index + step) % peers * width, axis=2
+            )
     token_rows = gathered.reshape(row_count, D)
     projected, mlp_units = input_folder(
         token_rows,

time: 608 us -> 575 us (0.946)
  waiting for transfers between devices: 408 us -> 361 us
  starting transfers between devices: 3.96 us -> 13.1 us
  local copies, waits for them, and re-layouts: 45.8 us -> 52.7 us
    all_gather x1, waiting for transfers between devices: 64.8 us -> 34.5 us  [shards(): lax.all_gather(up_weight, 'seq', axis=0, tiled=True)]
    all_gather x1 -> x0, waiting for transfers between devices: 23.5 us -> none  [shards(): gathered = lax.all_gather(normed, 'wblk', axis=2, tiled=True)]
    ppermute x0 -> x7, waiting for transfers between devices: none -> 20.3 us  [the longest x4 20.3 us: shards(): from_left = lax.ppermute(from_left, 'wblk', forward)]
    all_gather x1, waiting for transfers between devices: 13.8 us -> 0.01 us  [shards(): lax.all_gather(qkv_weight, 'seq', axis=0, tiled=True)]
    ppermute x0 -> x7, starting transfers between devices: none -> 9.17 us  [the longest x3 9.16 us: shards(): from_right = lax.ppermute(from_right, 'wblk', behind)]
    unnamed x16 -> x20, local copies, waits for them, and re-layouts: 26 us -> 26 us
    unnamed x9 -> x8, waiting for transfers between devices: 40 us -> 40 us
  transfers between devices with their start and end apart: 9 -> 15, of which waited for: 9 -> 11; matrix products, arithmetic and copies ran while one was open for 14% -> 16% of each run, Pallas kernels for 0% -> 0%
where the time goes in v1:
time: 575 us; the launch traced here: 573 us
  waiting for transfers between devices  361 us (63%)
  blocking collectives  59.7 us (10%)
  matrix products  52.8 us (9%)
  local copies, waits for them, and re-layouts  52.7 us (9%)
  other arithmetic  18.6 us (3%)
  between operations  15.3 us (3%)
  starting transfers between devices  13.1 us (2%)
    all_gather x1, waiting for transfers between devices, shards(): lax.all_gather(down_weight, 'seq', axis=1, tiled=True)  83 us
    all_gather x1, waiting for transfers between devices, shards(): key_piece = lax.all_gather(key_rows, 'seq', axis=1, tiled=True)  68.4 us
    all_gather x1, waiting for transfers between devices, shards(): value_piece = lax.all_gather(values, 'seq', axis=1, tiled=True)  59.5 us
    all_gather x1, waiting for transfers between devices, shards(): lax.all_gather(attn_weight, 'seq', axis=1, tiled=True)  50 us
    psum x1, blocking collectives, shards(): modulation = lax.psum(mod_terms.reshape(3, dim_local), 'seq')  44.7 us
    unnamed x8, waiting for transfers between devices  40 us
    all_gather x1, waiting for transfers between devices, shards(): lax.all_gather(up_weight, 'seq', axis=0, tiled=True)  34.5 us
    unnamed x20, local copies, waits for them, and re-layouts  26 us
  transfers between devices with their start and end apart: 15, of which 11 were waited for; matrix products, arithmetic and copies ran while one was open for 16% of the time, Pallas kernels for 0%

profile of v1, /device:TPU:2, one launch (start us, length us, event | category | flops | bytes accessed | tf_op | source)
XLA Modules:
  0.0 573.3 jit_solution(8886834452780840313)
XLA Ops:
  12.6 15.1 %all-reduce.2 = (f32[2,288]{1,0:T(2,128)S(1)}, f32[2,288]{1,0:T(2,128)S(1)}) all-reduce(f32[2,288]{1,0:T(2,128)S(1)} %get-tuple-element.6, f32[2,288]{1,0:T(2,128)S(1)} %get-tuple-element.5), channel_id=1, replica_groups=mesh['cfg'=2,'seq'=16,'wblk'=8] {'wblk'}, use_global_device_ids=true, to_apply=%region_4.5 | all-reduce | flops 1152 | bytes 9216 | tf_op jit(solution)/shard_map/psum | solution.py:122
  27.7 44.7 %psum.21 = f32[3,384]{1,0:T(4,128)S(1)} all-reduce(f32[3,384]{1,0:T(4,128)S(1)} %bitcast.105), channel_id=1, replica_groups=mesh['cfg'=2,'seq'=16,'wblk'=8] {'seq'}, use_global_device_ids=true, to_apply=%region_0.1 | all-reduce | flops 1152 | bytes 9216 | tf_op jit(solution)/shard_map/psum | solution.py:119
  78.6 6.0 %collective-permute-done = bf16[2,288,384]{2,1,0:T(8,128)(2,1)S(1)} collective-permute-done((bf16[2,288,384]{2,1,0:T(8,128)(2,1)S(1)}, bf16[2,288,384]{2,1,0:T(8,128)(2,1)S(1)}, u32[]{:S(2)}, u32[]{:S(2)}) %collective-permute-start) | collective-permute-done | bytes 442400 | tf_op jit(solution)/shard_map/ppermute | solution.py:138
  84.8 3.2 collective-permute-start.3
  88.4 5.1 collective-permute-done.2
  98.7 3.8 collective-permute-done.4
  106.0 5.4 collective-permute-done.6
  112.2 12.5 %copy.34 = bf16[3072,3,2,128]{0,3,2,1:T(8,128)(2,1)} copy(bf16[3072,3,2,128]{3,2,1,0:T(2,128)(2,1)} %all-gather.8.cloned.1.call-done) | data formatting | bytes 9437184 | tf_op jit(solution)/shard_map/reshape | solution.py:77
  124.8 6.8 %fusion.6 = f32[2,288,3,2,128]{4,1,3,2,0:T(8,128)S(1)} fusion(bf16[3072,3,2,128]{0,3,2,1:T(8,128)(2,1)} %copy.34, bf16[2,288,3072]{2,1,0:T(8,128)(2,1)} %constant_dynamic-update-slice_fusion), kind=kOutput, calls=%fused_computation.8 | convolution fusion | flops 2717908992 | bytes 10027008 | tf_op jit(solution)/shard_map/dot_general | solution.py:76
  140.5 34.5 %all-gather.14.cloned.1.call-done = bf16[3072,768]{1,0:T(8,128)(2,1)} async-done(((bf16[192,768]{1,0:T(8,128)(2,1)}), bf16[3072,768]{1,0:T(8,128)(2,1)}) %all-gather.14.cloned.1.call-update) | async-done | bytes 4718608 | tf_op jit(solution)/shard_map/all_gather | solution.py:152
  175.0 83.0 %all-gather.16.cloned.1.call-done = bf16[768,3072]{0,1:T(8,128)(2,1)} async-done(((bf16[768,192]{0,1:T(8,128)(2,1)}), bf16[768,3072]{0,1:T(8,128)(2,1)}) %all-gather.16.cloned.1.call-update) | async-done | bytes 4718608 | tf_op jit(solution)/shard_map/all_gather | solution.py:200
  258.0 15.0 %fusion.39 = f32[576,3072]{1,0:T(8,128)} fusion(bf16[768,3072]{0,1:T(8,128)(2,1)} %all-gather.16.cloned.1.call-done, bf16[576,3072]{1,0:T(8,128)(2,1)} %bitcast.18, bf16[3072,768]{1,0:T(8,128)(2,1)} %all-gather.14.cloned.1.call-done), kind=kOutput, calls=%fused_computation.34 | convolution fusion | flops 5439799296 | bytes 20054016 | tf_op jit(solution)/shard_map/dot_general | solution.py:85
  273.1 68.4 %all-gather.10.cloned.1.call-done = bf16[2,4608,2,128]{3,1,2,0:T(8,128)(2,1)} async-done(((bf16[2,288,2,128]{3,1,2,0:T(8,128)(2,1)}), bf16[2,4608,2,128]{3,1,2,0:T(8,128)(2,1)}) %all-gather.10.cloned.1.call-update) | async-done | bytes 4718608 | tf_op jit(solution)/shard_map/all_gather | solution.py:169
  341.5 13.6 %fusion = (f32[2,2,288]{2,1,0:T(2,128)S(1)}, f32[2,2,288,4608]{3,2,1,0:T(8,128)}) fusion(pred[2,4608]{1,0:T(4,128)(4,1)S(1)} %compare_or_fusion, bf16[2,4608,2,128]{3,1,2,0:T(8,128)(2,1)} %all-gather.10.cloned.1.call-done, bf16[2,288,2,128]{1,2,3,0:T(2,128)(2,1)S(1)} %bitcast.100), kind=kOutput, calls=%fused_computation.2 | convolution fusion | flops 1374878592 | bytes 26260992 | tf_op jit(solution)/shard_map/pqhd,pkhd->phqk/dot_general | solution.py:178
  355.0 10.3 %fusion.1 = f32[2,2,288]{2,1,0:T(2,128)S(1)} fusion(f32[2,2,288,4608]{3,2,1,0:T(8,128)} %get-tuple-element.31, f32[2,2,288]{2,1,0:T(2,128)S(1)} %broadcast_maximum_fusion, pred[2,4608]{1,0:T(4,128)(4,1)S(1)} %compare_or_fusion), kind=kLoop, calls=%fused_computation.3 | loop fusion | flops 21232512 | bytes 21252096 | tf_op jit(solution)/shard_map/reduce_sum | solution.py:184
  365.4 59.5 %all-gather.18.cloned.1.call-done = bf16[2,4608,1,2,128]{4,1,3,2,0:T(8,128)(2,1)} async-done(((bf16[2,288,1,2,128]{4,1,3,2,0:T(8,128)(2,1)}), bf16[2,4608,1,2,128]{4,1,3,2,0:T(8,128)(2,1)}) %all-gather.18.cloned.1.call-update) | async-done | bytes 4718608 | tf_op jit(solution)/shard_map/all_gather | solution.py:170
  424.9 10.9 %fusion.28 = bf16[2,288,2,128]{3,1,2,0:T(8,128)(2,1)S(1)} fusion(bf16[2,4608,1,2,128]{4,1,3,2,0:T(8,128)(2,1)} %all-gather.18.cloned.1.call-done, f32[2,2,288,4608]{3,2,1,0:T(8,128)} %get-tuple-element.31, f32[2,2,288]{2,1,0:T(2,128)S(1)} %broadcast_maximum_fusion, pred[2,4608]{1,0:T(4,128)(4,1)S(1)} %compare_or_fusion, f32[2,288,2]{1,2,0:T(2,128)S(1)} %bitcast.106), kind=kOutput, calls=%fused_computation.27 | convolution fusion | flops 1380483072 | bytes 26265600 | tf_op jit(solution)/shard_map/phqk,pkhd->phqd/dot_general | solution.py:185
  436.0 50.0 %all-gather.12.cloned.1.call-done = bf16[256,3072]{0,1:T(8,128)(2,1)} async-done(((bf16[256,192]{0,1:T(8,128)(2,1)}), bf16[256,3072]{0,1:T(8,128)(2,1)}) %all-gather.12.cloned.1.call-update) | async-done | bytes 1572880 | tf_op jit(solution)/shard_map/all_gather | solution.py:199
  486.1 6.4 %add_convert_fusion = bf16[576,3072]{1,0:T(8,128)(2,1)} fusion(f32[576,3072]{1,0:T(8,128)} %fusion.39, bf16[256,3072]{0,1:T(8,128)(2,1)} %all-gather.12.cloned.1.call-done, bf16[72,8,2,128]{3,2,1,0:T(2,128)(2,1)S(1)} %bitcast.101), kind=kOutput, calls=%fused_computation.7 | convolution fusion | flops 909508608 | bytes 12484608 | tf_op jit(solution)/shard_map/dot_general | solution.py:84
  492.5 12.3 %copy.35 = bf16[2,288,3072]{1,0,2:T(2,128)(2,1)} copy(bf16[2,288,3072]{2,1,0:T(8,128)(2,1)} %bitcast.95) | data formatting | bytes 7077888
  504.8 10.1 %reshape.323 = bf16[3072,576]{1,0:T(8,128)(2,1)} reshape(bf16[3072,2,288]{2,1,0:T(2,128)(2,1)} %bitcast.94) | data formatting | bytes 7077888
  514.9 37.4 %reduce-scatter.4.cloned.1.call-done = bf16[384,576]{1,0:T(8,128)(2,1)} async-done(((bf16[3072,576]{1,0:T(8,128)(2,1)}), bf16[384,576]{1,0:T(8,128)(2,1)}) %reduce-scatter.4.cloned.1.call-update) | async-done | bytes 442384
  556.1 3.5 all-to-all-start
  560.2 5.2 all-to-all-done
  (91 shorter events, 35.3 us)
Async XLA Ops:
  7.2 3.9 copy-start
  7.2 67.3 %copy-start.4 = (bf16[1,2,32,384]{3,2,1,0:T(8,128)(2,1)S(1)}, bf16[1,2,32,384]{3,2,1,0:T(8,128)(2,1)}, u32[]{:S(2)}) copy-start(bf16[1,2,32,384]{3,2,1,0:T(8,128)(2,1)} %param.12) | copy-start | bytes 147460
  7.2 67.3 %copy-start.2 = (bf16[2,256,384]{2,1,0:T(8,128)(2,1)S(1)}, bf16[2,256,384]{2,1,0:T(8,128)(2,1)}, u32[]{:S(2)}) copy-start(bf16[2,256,384]{2,1,0:T(8,128)(2,1)} %param.13) | copy-start | bytes 1179652
  7.2 80.9 %copy-start.5 = (f32[128]{0:T(128)S(1)}, f32[128]{0:T(128)}, u32[]{:S(2)}) copy-start(f32[128]{0:T(128)} %param.19) | copy-start | bytes 1540
  7.2 81.0 %copy-start.6 = (f32[128]{0:T(128)S(1)}, f32[128]{0:T(128)}, u32[]{:S(2)}) copy-start(f32[128]{0:T(128)} %param.18) | copy-start | bytes 1540
  7.2 105.0 %all-gather.8.cloned.1.call-start = ((), (), s32[]{:S(2)}) async-start(), calls=%async_computation.2 | async-start | bytes 5013504 | tf_op jit(solution)/shard_map/all_gather | solution.py:151
  8.0 167.1 %all-gather.14.cloned.1.call-start = ((), (), s32[]{:S(2)}) async-start(), calls=%async_computation.5 | async-start | bytes 5013504 | tf_op jit(solution)/shard_map/all_gather | solution.py:152
  8.7 249.3 %all-gather.16.cloned.1.call-start = ((), (), s32[]{:S(2)}) async-start(), calls=%async_computation.6 | async-start | bytes 5013504 | tf_op jit(solution)/shard_map/all_gather | solution.py:200
  9.4 332.0 %all-gather.10.cloned.1.call-start = ((), (), s32[]{:S(2)}) async-start(), calls=%async_computation.3 | async-start | bytes 5013504 | tf_op jit(solution)/shard_map/all_gather | solution.py:169
  75.6 8.9 %collective-permute-start = (bf16[2,288,384]{2,1,0:T(8,128)(2,1)S(1)}, bf16[2,288,384]{2,1,0:T(8,128)(2,1)S(1)}, u32[]{:S(2)}, u32[]{:S(2)}) collective-permute-start(bf16[2,288,384]{2,1,0:T(8,128)(2,1)S(1)} %get-tuple-element.15), channel_id=1, source_target_pairs={{0,1},{1,2},{2,3},{3,4},{4,5},{5,6},{6,7},{7,0},{8,9},{9,10},{10,1... | collective-permute-start | bytes 1327112 | tf_op jit(solution)/shard_map/ppermute | solution.py:138
  75.6 9.1 %collective-permute-start.1 = (bf16[2,288,384]{2,1,0:T(8,128)(2,1)S(1)}, bf16[2,288,384]{2,1,0:T(8,128)(2,1)S(1)}, u32[]{:S(2)}, u32[]{:S(2)}) collective-permute-start(bf16[2,288,384]{2,1,0:T(8,128)(2,1)S(1)} %get-tuple-element.15), channel_id=1, source_target_pairs={{0,7},{1,0},{2,1},{3,2},{4,3},{5,4},{6,5},{7,6},{8,15},{9,8},{10,9... | collective-permute-start | bytes 1327112 | tf_op jit(solution)/shard_map/ppermute | solution.py:143
  84.6 8.9 %collective-permute-start.2 = (bf16[2,288,384]{2,1,0:T(8,128)(2,1)S(1)}, bf16[2,288,384]{2,1,0:T(8,128)(2,1)S(1)}, u32[]{:S(2)}, u32[]{:S(2)}) collective-permute-start(bf16[2,288,384]{2,1,0:T(8,128)(2,1)S(1)} %collective-permute-done), channel_id=1, source_target_pairs={{0,1},{1,2},{2,3},{3,4},{4,5},{5,6},{6,7},{7,0},{8,9},{9,10},{10,1... | collective-permute-start | bytes 1327112 | tf_op jit(solution)/shard_map/ppermute | solution.py:138
  84.8 10.0 %collective-permute-start.3 = (bf16[2,288,384]{2,1,0:T(8,128)(2,1)S(1)}, bf16[2,288,384]{2,1,0:T(8,128)(2,1)S(1)}, u32[]{:S(2)}, u32[]{:S(2)}) collective-permute-start(bf16[2,288,384]{2,1,0:T(8,128)(2,1)S(1)} %collective-permute-done.1), channel_id=1, source_target_pairs={{0,7},{1,0},{2,1},{3,2},{4,3},{5,4},{6,5},{7,6},{8,15},{9,8},{10,9... | collective-permute-start | bytes 1327112 | tf_op jit(solution)/shard_map/ppermute | solution.py:143
  93.5 8.9 %collective-permute-start.4 = (bf16[2,288,384]{2,1,0:T(8,128)(2,1)S(1)}, bf16[2,288,384]{2,1,0:T(8,128)(2,1)S(1)}, u32[]{:S(2)}, u32[]{:S(2)}) collective-permute-start(bf16[2,288,384]{2,1,0:T(8,128)(2,1)S(1)} %collective-permute-done.2), channel_id=1, source_target_pairs={{0,1},{1,2},{2,3},{3,4},{4,5},{5,6},{6,7},{7,0},{8,9},{9,10},{10,1... | collective-permute-start | bytes 1327112 | tf_op jit(solution)/shard_map/ppermute | solution.py:138
  94.8 10.3 %collective-permute-start.5 = (bf16[2,288,384]{2,1,0:T(8,128)(2,1)S(1)}, bf16[2,288,384]{2,1,0:T(8,128)(2,1)S(1)}, u32[]{:S(2)}, u32[]{:S(2)}) collective-permute-start(bf16[2,288,384]{2,1,0:T(8,128)(2,1)S(1)} %collective-permute-done.3), channel_id=1, source_target_pairs={{0,7},{1,0},{2,1},{3,2},{4,3},{5,4},{6,5},{7,6},{8,15},{9,8},{10,9... | collective-permute-start | bytes 1327112 | tf_op jit(solution)/shard_map/ppermute | solution.py:143
  102.4 8.9 %collective-permute-start.6 = (bf16[2,288,384]{2,1,0:T(8,128)(2,1)S(1)}, bf16[2,288,384]{2,1,0:T(8,128)(2,1)S(1)}, u32[]{:S(2)}, u32[]{:S(2)}) collective-permute-start(bf16[2,288,384]{2,1,0:T(8,128)(2,1)S(1)} %collective-permute-done.4), channel_id=1, source_target_pairs={{0,1},{1,2},{2,3},{3,4},{4,5},{5,6},{6,7},{7,0},{8,9},{9,10},{10,1... | collective-permute-start | bytes 1327112 | tf_op jit(solution)/shard_map/ppermute | solution.py:138
  131.5 1.2 copy-start.3
  133.2 6.6 %copy-start.7 = (s32[2]{0:T(128)S(1)}, s32[2]{0:T(128)}, u32[]{:S(2)}) copy-start(s32[2]{0:T(128)} %param.22) | copy-start | bytes 28
  137.1 287.8 %all-gather.18.cloned.1.call-start = ((), (), s32[]{:S(2)}) async-start(), calls=%async_computation.7 | async-start | bytes 5013504 | tf_op jit(solution)/shard_map/all_gather | solution.py:170
  139.0 347.1 %all-gather.12.cloned.1.call-start = ((), (), s32[]{:S(2)}) async-start(), calls=%async_computation.4 | async-start | bytes 1671168 | tf_op jit(solution)/shard_map/all_gather | solution.py:199
  139.5 412.8 %reduce-scatter.4.cloned.1.call-start = ((), (), s32[]{:S(2)}) async-start(), calls=%async_computation.8 | async-start | bytes 4423680
  514.9 51.5 %copy-start.1 = (bf16[192,3,384]{2,0,1:T(8,128)(2,1)S(1)}, bf16[192,3,384]{2,0,1:T(8,128)(2,1)}, u32[]{:S(2)}) copy-start(bf16[192,3,384]{2,0,1:T(8,128)(2,1)} %param.15) | copy-start | bytes 1327108
  556.1 9.3 %all-to-all-start = ((bf16[2,1,256,384]{3,2,1,0:T(8,128)(2,1)}), bf16[2,1,256,384]{3,2,1,0:T(8,128)(2,1)S(1)}, u32[]{:S(2)}, u32[]{:S(2)}) async-start(bf16[2,1,256,384]{3,2,1,0:T(8,128)(2,1)} %slice_bitcast_fusion.2), calls=%async_computation | async-start | bytes 786432 | tf_op jit(solution)/shard_map/all_to_all | solution.py:212
Sparse Core Ops, SparseCore 0:
  10.5 81.4 all-gather.7
  94.4 80.5 all-gather.13
  177.5 80.5 all-gather.15
  260.9 80.5 all-gather.9
  344.3 80.5 all-gather.17
  427.2 58.8 all-gather.11
  515.1 37.2 reduce-scatter.3
